TPU v7x, 512 devices: a whole 4x8x8 slice. The times are simulated.
512 devices in a mesh: seq: 64 (over z, x, core), head: 8 (over y).
Axes of the slice: x: 4, y: 8, z: 8, core: 2. Of those that a mesh axis runs over, the one named last changes fastest.
Arguments:
- projected: float32 [65536, 2560], P(('seq', 'head')), may hold values from -6 to 6
- out_grads: float32 [65536, 2048], P(('seq', 'head')), may hold values from -6 to 6
- conv_weight: float32 [3, 2560], replicated, may hold values from -2.4 to 2.4
- doc_lengths: int32 [16], replicated, may hold values from 1 to 32768, 65536 in all
Outputs:
- grad_projected: float32 [65536, 2560], P(('seq', 'head'))
- grad_conv: float32 [3, 2560], replicated
Inputs may be any that keep to these rules, and one draw needn't show every extreme that they name: `doc_lengths`: the 16 documents fill the 65536 tokens end to end; the longest holds exactly half of 65536 tokens.
All inputs are finite; a program needn't handle non-finite values.
Results may differ from a plain program's by a relative error of at most 0.0003.
Values sent between devices are 32-bit elements; how exact they have to be, the bound alone decides.
No kernel may reach another device: no remote copies, remote signals or barrier semaphores. Data moves between devices by JAX's collectives and lax.ppermute only.
A program may use at most 128 MiB of HBM per device.

v0:
```python
import math
import jax
import jax.numpy as jnp
import numpy as np
from jax import lax
from jax.sharding import PartitionSpec as P

KEY_DIM = 16
HEAD_DIM = 128
HIGHEST = lax.Precision.HIGHEST


def carried_in(x, axis, combine, identity, reverse):
    length, here = (lax.axis_size(axis), lax.axis_index(axis))
    everything = jax.tree.map(lambda part: lax.all_gather(part, axis), x)
    start = jax.tree.map(
        lambda part, zero: jnp.broadcast_to(jnp.asarray(zero, part.dtype), part.shape), x, identity
    )

    def lap(k, before):
        at = length - 1 - k if reverse else k
        reached = at > here if reverse else at < here
        new = combine(before, jax.tree.map(lambda part: part[at], everything))
        return jax.tree.map(lambda a, b: jnp.where(reached, a, b), new, before)

    return lax.fori_loop(0, length, lap, start)


def passed_along(value, axis, steps):
    count = lax.axis_size(axis)
    initial, last = (max(0, -steps), min(count, count - steps))
    return lax.ppermute(value, axis, [(source, source + steps) for source in range(initial, last)])


def feature_map(columns):
    key_size = columns.shape[1]
    upper_i, upper_j = np.triu_indices(key_size)
    factors = np.where(upper_i == upper_j, 1.0 / math.sqrt(2.0), 1.0).astype(np.float32)
    products = columns[:, upper_i, :] * columns[:, upper_j, :] * jnp.asarray(factors)[None, :, None]
    constant = jnp.ones((columns.shape[0], 1, columns.shape[2]), jnp.float32)
    return jnp.concatenate([constant, columns, products], axis=1)


def doc_place(doc_lengths, anchor, amount):
    positions = anchor + jnp.arange(amount, dtype=jnp.int32)
    starts = jnp.cumsum(doc_lengths) - doc_lengths
    begins = jnp.max(jnp.where(starts[None, :] <= positions[:, None], starts[None, :], 0), axis=1)
    return (begins, positions - begins)


def conv_forward(signal, leading, weights, offsets):
    row_count = signal.shape[0]
    behind = jnp.concatenate([leading, signal], axis=0)
    back_one = behind[1 : row_count + 1] * (offsets[0:row_count] >= 1).astype(jnp.float32)[:, None]
    back_two = behind[0:row_count] * (offsets[0:row_count] >= 2).astype(jnp.float32)[:, None]
    return weights[0] * signal + weights[1] * back_one + weights[2] * back_two


def conv_backward(grad_rows, trailing, signal, leading, weights, offsets):
    row_count = grad_rows.shape[0]
    ahead_rows = jnp.concatenate([grad_rows, trailing], axis=0)
    ahead_one = (
        ahead_rows[1 : row_count + 1]
        * (offsets[1 : row_count + 1] >= 1).astype(jnp.float32)[:, None]
    )
    ahead_two = (
        ahead_rows[2 : row_count + 2]
        * (offsets[2 : row_count + 2] >= 2).astype(jnp.float32)[:, None]
    )
    grad_signal = weights[0] * grad_rows + weights[1] * ahead_one + weights[2] * ahead_two
    behind = jnp.concatenate([leading, signal], axis=0)
    own_one = (offsets[0:row_count] >= 1).astype(jnp.float32)[:, None]
    own_two = (offsets[0:row_count] >= 2).astype(jnp.float32)[:, None]
    grad_weights = jnp.stack(
        [
            jnp.sum(grad_rows * signal, axis=0),
            jnp.sum(grad_rows * behind[1 : row_count + 1] * own_one, axis=0),
            jnp.sum(grad_rows * behind[0:row_count] * own_two, axis=0),
        ],
        axis=0,
    )
    return (grad_signal, grad_weights)


def combine(earlier, following):
    carry_keep = 1.0 - following[2]
    return (
        following[0] + carry_keep[:, None, None] * earlier[0],
        following[1] + carry_keep[:, None] * earlier[1],
        jnp.maximum(earlier[2], following[2]),
    )


def attention_grads(mixed_rows, out_flat, begins, stretch_start):
    length = mixed_rows.shape[0]
    head_width = 2 * KEY_DIM + HEAD_DIM
    local_heads = mixed_rows.shape[1] // head_width
    block_len = min(128, length)
    blocks = length // block_len
    scale_key = KEY_DIM ** (-0.25)
    shaped = mixed_rows.reshape(length, local_heads, head_width)
    query_cols = jnp.transpose(shaped[:, :, :KEY_DIM], (1, 2, 0)) * scale_key
    key_cols = jnp.transpose(shaped[:, :, KEY_DIM : 2 * KEY_DIM], (1, 2, 0)) * scale_key
    values = shaped[:, :, 2 * KEY_DIM :]
    upstream = out_flat.reshape(length, local_heads, HEAD_DIM)
    query_feat, query_pull = jax.vjp(feature_map, query_cols)
    key_feat, key_pull = jax.vjp(feature_map, key_cols)
    feat_count = query_feat.shape[1]
    last_begin = begins[length - 1]
    has_start = (last_begin >= stretch_start).astype(jnp.float32).reshape(1)
    tail_mask = (begins == last_begin).astype(jnp.float32)
    tail_feat = key_feat * tail_mask[None, None, :]
    tail_state = jnp.einsum("hfl,lhe->hfe", tail_feat, values, precision=HIGHEST)
    tail_norm = jnp.sum(tail_feat, axis=2)
    identity = (jnp.zeros_like(tail_state), jnp.zeros_like(tail_norm), jnp.zeros((1,), jnp.float32))
    prefix = carried_in((tail_state, tail_norm, has_start), "seq", combine, identity, False)
    causal = jnp.arange(block_len)[:, None] >= jnp.arange(block_len)[None, :]
    indices = jnp.arange(blocks, dtype=jnp.int32)

    def forward_block(carried, block_index):
        carry_state, carry_norm = carried
        offset_rows = block_index * block_len
        block_start = stretch_start + offset_rows
        query_blk = lax.dynamic_slice_in_dim(query_feat, offset_rows, block_len, 2)
        key_blk = lax.dynamic_slice_in_dim(key_feat, offset_rows, block_len, 2)
        value_blk = lax.dynamic_slice_in_dim(values, offset_rows, block_len, 0)
        doc_blk = lax.dynamic_slice_in_dim(begins, offset_rows, block_len, 0)
        allowed = causal & (doc_blk[:, None] == doc_blk[None, :])
        scores = jnp.where(
            allowed[None], jnp.einsum("hft,hfs->hts", query_blk, key_blk, precision=HIGHEST), 0.0
        )
        from_carry = (doc_blk < block_start).astype(jnp.float32)
        numerator = jnp.einsum("hts,she->the", scores, value_blk, precision=HIGHEST) + from_carry[
            :, None, None
        ] * jnp.einsum("hft,hfe->the", query_blk, carry_state, precision=HIGHEST)
        denominator = jnp.sum(scores, axis=2) + from_carry[None, :] * jnp.einsum(
            "hft,hf->ht", query_blk, carry_norm, precision=HIGHEST
        )
        block_tail = (doc_blk == doc_blk[block_len - 1]).astype(jnp.float32)
        carry_keep = (doc_blk[block_len - 1] < block_start).astype(jnp.float32)
        tail_keys = key_blk * block_tail[None, None, :]
        next_state = (
            jnp.einsum("hfs,she->hfe", tail_keys, value_blk, precision=HIGHEST)
            + carry_keep * carry_state
        )
        next_norm = jnp.sum(tail_keys, axis=2) + carry_keep * carry_norm
        return ((next_state, next_norm), (numerator, denominator, carry_state, carry_norm, scores))

    forward_out = lax.scan(forward_block, (prefix[0], prefix[1]), indices)
    numerators, denominators, states, norms, kept_scores = forward_out[1]
    denom_rows = jnp.transpose(denominators, (0, 2, 1)).reshape(length, local_heads)
    attended = numerators.reshape(length, local_heads, HEAD_DIM) / denom_rows[:, :, None]
    grad_num = upstream / denom_rows[:, :, None]
    scalar_grad = -jnp.sum(upstream * attended, axis=2) / denom_rows
    lead_mask = (begins < stretch_start).astype(jnp.float32)
    lead_feat = query_feat * lead_mask[None, None, :]
    lead_state = jnp.einsum("hfl,lhe->hfe", lead_feat, grad_num, precision=HIGHEST)
    lead_norm = jnp.einsum("hfl,lh->hf", lead_feat, scalar_grad, precision=HIGHEST)
    suffix = carried_in((lead_state, lead_norm, has_start), "seq", combine, identity, True)

    def backward_block(carried, inputs):
        back_state, back_norm = carried
        block_index, carry_state, carry_norm, scores = inputs
        offset_rows = block_index * block_len
        block_start = stretch_start + offset_rows
        query_blk = lax.dynamic_slice_in_dim(query_feat, offset_rows, block_len, 2)
        key_blk = lax.dynamic_slice_in_dim(key_feat, offset_rows, block_len, 2)
        value_blk = lax.dynamic_slice_in_dim(values, offset_rows, block_len, 0)
        doc_blk = lax.dynamic_slice_in_dim(begins, offset_rows, block_len, 0)
        grad_blk = lax.dynamic_slice_in_dim(grad_num, offset_rows, block_len, 0)
        scalar_blk = lax.dynamic_slice_in_dim(scalar_grad, offset_rows, block_len, 0)
        scalar_cols = scalar_blk.T
        allowed = causal & (doc_blk[:, None] == doc_blk[None, :])
        dscores = jnp.where(
            allowed[None],
            jnp.einsum("the,she->hts", grad_blk, value_blk, precision=HIGHEST)
            + scalar_cols[:, :, None],
            0.0,
        )
        from_carry = (doc_blk < block_start).astype(jnp.float32)
        block_tail = (doc_blk == doc_blk[block_len - 1]).astype(jnp.float32)
        carry_keep = (doc_blk[block_len - 1] < block_start).astype(jnp.float32)
        grad_query = jnp.einsum("hts,hfs->hft", dscores, key_blk, precision=HIGHEST) + from_carry[
            None, None, :
        ] * (
            jnp.einsum("hfe,the->hft", carry_state, grad_blk, precision=HIGHEST)
            + carry_norm[:, :, None] * scalar_cols[:, None, :]
        )
        grad_key = jnp.einsum("hts,hft->hfs", dscores, query_blk, precision=HIGHEST) + block_tail[
            None, None, :
        ] * (
            jnp.einsum("hfe,she->hfs", back_state, value_blk, precision=HIGHEST)
            + back_norm[:, :, None]
        )
        grad_value = jnp.einsum("hts,the->she", scores, grad_blk, precision=HIGHEST) + block_tail[
            :, None, None
        ] * jnp.einsum("hfs,hfe->she", key_blk, back_state, precision=HIGHEST)
        lead_blk = query_blk * from_carry[None, None, :]
        next_state = (
            jnp.einsum("hft,the->hfe", lead_blk, grad_blk, precision=HIGHEST)
            + carry_keep * back_state
        )
        next_norm = (
            jnp.einsum("hft,th->hf", lead_blk, scalar_blk, precision=HIGHEST)
            + carry_keep * back_norm
        )
        return ((next_state, next_norm), (grad_query, grad_key, grad_value))

    swept_back = lax.scan(
        backward_block, (suffix[0], suffix[1]), (indices, states, norms, kept_scores), reverse=True
    )
    grad_qblocks, grad_kblocks, grad_vblocks = swept_back[1]
    query_grad = jnp.transpose(grad_qblocks, (1, 2, 0, 3)).reshape(local_heads, feat_count, length)
    key_grad = jnp.transpose(grad_kblocks, (1, 2, 0, 3)).reshape(local_heads, feat_count, length)
    value_grad = grad_vblocks.reshape(length, local_heads, HEAD_DIM)
    query_in = jnp.transpose(query_pull(query_grad)[0] * scale_key, (2, 0, 1))
    key_in = jnp.transpose(key_pull(key_grad)[0] * scale_key, (2, 0, 1))
    return jnp.concatenate([query_in, key_in, value_grad], axis=2).reshape(
        length, local_heads * head_width
    )


def on_device(projected, out_grads, conv_weight, doc_lengths):
    row_count = projected.shape[0]
    head_count = lax.axis_size("head")
    seq_index = lax.axis_index("seq")
    head_index = lax.axis_index("head")
    group_len = row_count * head_count
    token_base = (seq_index * head_count + head_index) * row_count
    stretch_start = seq_index * group_len
    token_begins, token_offsets = doc_place(doc_lengths, token_base, row_count + 2)
    leading = passed_along(projected[row_count - 2 :], ("seq", "head"), 1)
    outgoing = conv_forward(projected, leading, conv_weight, token_offsets)
    arrived, upstream = (
        lax.all_to_all(outgoing, "head", split_axis=1, concat_axis=0, tiled=True),
        lax.all_to_all(out_grads, "head", split_axis=1, concat_axis=0, tiled=True),
    )
    group_begins, group_offsets = doc_place(doc_lengths, stretch_start, group_len + 2)
    grad_mixed = attention_grads(arrived, upstream, group_begins[:group_len], stretch_start)
    returned = lax.all_to_all(grad_mixed, "head", split_axis=0, concat_axis=1, tiled=True)
    trailing = passed_along(returned[:2], ("seq", "head"), -1)
    grad_projected, weight_part = conv_backward(
        returned, trailing, projected, leading, conv_weight, token_offsets
    )
    grad_conv = lax.psum(weight_part, ("seq", "head"))
    return (grad_projected, grad_conv)


def solution(mesh):
    return jax.shard_map(
        on_device,
        mesh=mesh,
        in_specs=(P(("seq", "head"), None), P(("seq", "head"), None), P(), P()),
        out_specs=(P(("seq", "head"), None), P()),
        check_vma=False,
    )
```

profile of v0, /device:TPU:1, one launch (start us, length us, event | category | flops | bytes accessed | tf_op | source)
XLA Modules:
  0.0 1203.6 jit_solution(1783652886522364890)
XLA Ops:
  20.8 6.1 all-to-all-start
  28.4 33.2 %all-to-all-done = f32[128,8,320]{0,2,1:T(8,128)S(1)} async-done(((f32[128,8,320]{0,2,1:T(8,128)}), f32[128,8,320]{0,2,1:T(8,128)S(1)}, u32[]{:S(2)}, u32[]{:S(2)}) %all-to-all-start) | async-done | bytes 1310752 | tf_op jit(solution)/shard_map/all_to_all | solution.py:235
  76.8 4.8 broadcast_multiply_fusion.1
  91.7 131.3 %all-reduce = f32[64]{0:T(128)S(1)} all-reduce(f32[64]{0:T(128)S(1)} %dynamic-update-slice), channel_id=1, replica_groups=mesh['seq'=64,'head'=8] {'seq'}, use_global_device_ids=true, to_apply=%add | all-reduce | flops 64 | bytes 512
  232.5 51.4 %all-gather.4 = f32[64,2,153]{2,1,0:T(2,128)S(1)} all-gather(f32[1,2,153]{2,1,0:T(2,128)S(1)} %copy.127), channel_id=3, replica_groups=mesh['seq'=64,'head'=8] {'seq'}, dimensions={0}, use_global_device_ids=true | all-gather | bytes 79560 | tf_op jit(solution)/shard_map/all_gather | solution.py:15
  283.9 187.7 %while.82 = (s32[]{:T(128)}, f32[2,153,128]{2,1,0:T(8,128)S(1)}, f32[2,153]{1,0:T(2,128)S(1)}, s32[]{:T(128)}, f32[64,2,153,128]{3,2,1,0:T(8,128)}, /*index=5*/f...) while((s32[]{:T(128)}, f32[2,153,128]{2,1,0:T(8,128)S(1)}, ...), condition=%wide.region_5.6_spmd.clone, body=%wide.region_4.5_spmd.clone.sunk | while | flops 157901 | bytes 473831 | solution.py:26
  472.9 110.3 %while.80 = (s32[]{:T(128)}, f32[2,153,128]{2,1,0:T(8,128)S(1)}, f32[2,153]{1,0:T(2,128)S(1)}, f32[8,128,2,128]{1,0,3,2:T(8,128)}, f32[8,2,128]{2,1,0:T(2,128)S(...) while((s32[]{:T(128)}, f32[2,153,128]{2,1,0:T(8,128)S(1)}, ...), condition=%wide.region_9.10_spmd.clone, body=%wide.region_6.9_spmd.clone.sunk | while | flops 231664960 | bytes 3280461 | solution.py:149
  490.7 4.8 dynamic_update_slice.74
  504.5 4.8 dynamic_update_slice.74
  518.3 4.8 dynamic_update_slice.74
  532.1 4.8 dynamic_update_slice.74
  545.9 4.8 dynamic_update_slice.74
  573.4 4.8 dynamic_update_slice.74
  593.5 49.5 %all-gather.5 = f32[64,2,153]{2,1,0:T(2,128)S(1)} all-gather(f32[1,2,153]{2,1,0:T(2,128)S(1)} %bitcast.282), channel_id=5, replica_groups=mesh['seq'=64,'head'=8] {'seq'}, dimensions={0}, use_global_device_ids=true | all-gather | bytes 79560 | tf_op jit(solution)/shard_map/all_gather | solution.py:15
  643.0 36.5 %all-gather.11.cloned.1.call-done = f32[128,153,128]{2,1,0:T(8,128)} async-done(((f32[2,153,128]{2,1,0:T(8,128)}), f32[128,153,128]{2,1,0:T(8,128)}) %all-gather.11.cloned.1.call-update) | async-done | bytes 10027024 | tf_op jit(solution)/shard_map/all_gather | solution.py:15
  679.5 195.2 %while.83 = (s32[]{:T(128)}, f32[2,153,128]{2,1,0:T(8,128)S(1)}, f32[2,153]{1,0:T(2,128)S(1)}, s32[]{:T(128)}, f32[64,2,153,128]{3,2,1,0:T(8,128)}, /*index=5*/f...) while((s32[]{:T(128)}, f32[2,153,128]{2,1,0:T(8,128)S(1)}, ...), condition=%wide.region_12.13_spmd.clone, body=%wide.region_11.12_spmd.clone.sunk | while | flops 157905 | bytes 473893 | solution.py:26
  878.2 112.1 %while.81 = (s32[]{:T(128)}, f32[2,153,128]{2,1,0:T(8,128)S(1)}, f32[2,153]{1,0:T(2,128)S(1)}, f32[8,2,153,128]{3,2,1,0:T(8,128)}, f32[8,2,153,128]{3,2,1,0:T(8,...) while((s32[]{:T(128)}, f32[2,153,128]{2,1,0:T(8,128)S(1)}, ...), condition=%wide.region_14.15_spmd.clone, body=%wide.region_13.14_spmd.clone.sunk | while | flops 462717824 | bytes 4866477 | solution.py:209
  998.9 5.9 fusion.90
  1004.9 14.0 %scatter_fusion = f32[2,16,1024]{2,0,1:T(2,128)S(1)} fusion(f32[2,16,1024]{2,0,1:T(2,128)S(1)} %split.16, s32[136]{0:T(256)S(1)} %copy-done.23, f32[136,2,1024]{2,1,0:T(2,128)} %get-tuple-element.1103), kind=kCustom, calls=%fused_computation.4 | custom fusion | flops 278528 | bytes 3342880 | tf_op jit(solution)/shard_map/transpose(jvp())/scatter-add | solution.py:39
  1018.9 7.6 scatter_fusion.1
  1027.7 7.6 scatter_fusion.3
  1035.3 7.6 scatter_fusion.2
  1048.3 40.7 %all_to_all.51 = f32[8,128,320]{1,2,0:T(8,128)S(1)} all-to-all(f32[8,128,320]{1,2,0:T(8,128)S(1)} %copy.143), channel_id=1, replica_groups=mesh['seq'=64,'head'=8] {'head'}, dimensions={0} | all-to-all | bytes 2621440 | tf_op jit(solution)/shard_map/all_to_all | solution.py:240
  1093.7 95.5 %psum.7 = f32[3,2560]{1,0:T(4,128)} all-reduce(f32[3,2560]{1,0:T(4,128)S(1)} %pad_maximum_fusion.5), channel_id=1, replica_groups=mesh['seq'=64,'head'=8] {'seq','head'}, use_global_device_ids=true, to_apply=%region_22.23 | all-reduce | flops 7680 | bytes 61440 | tf_op jit(solution)/shard_map/psum | solution.py:245
  (838 shorter events, 642.5 us)
Async XLA Ops:
  8.1 9.1 collective-permute-start
  17.2 3.6 copy-start.3
  20.8 6.9 copy-start.24
  20.8 6.9 copy-start.23
  20.8 40.9 %all-to-all-start = ((f32[128,8,320]{0,2,1:T(8,128)}), f32[128,8,320]{0,2,1:T(8,128)S(1)}, u32[]{:S(2)}, u32[]{:S(2)}) async-start(f32[128,8,320]{0,2,1:T(8,128)} %bitcast.265), calls=%async_computation | async-start | bytes 2621440 | tf_op jit(solution)/shard_map/all_to_all | solution.py:235
  26.9 257.1 %all-gather.9.cloned.1.call-start = ((), (), s32[]{:S(2)}) async-start(), calls=%async_computation.3 | async-start | bytes 10649600 | tf_op jit(solution)/shard_map/all_gather | solution.py:15
  27.0 62.6 %copy-start.22 = (s32[1026]{0:T(1024)}, s32[1026]{0:T(1024)S(1)}, u32[]{:S(2)}) copy-start(s32[1026]{0:T(1024)S(1)} %select_reduce_fusion) | copy-start | bytes 12316
  64.6 9.1 copy-start.7
  85.3 137.7 %all-to-all-start.1 = ((f32[128,8,256]{0,2,1:T(8,128)}), f32[128,8,256]{0,2,1:T(8,128)S(1)}, u32[]{:S(2)}, u32[]{:S(2)}) async-start(f32[128,8,256]{0,2,1:T(8,128)} %bitcast.273), calls=%async_computation.1 | async-start | bytes 2097152 | tf_op jit(solution)/shard_map/all_to_all | solution.py:236
  88.8 590.7 %all-gather.11.cloned.1.call-start = ((), (), s32[]{:S(2)}) async-start(), calls=%async_computation.4 | async-start | bytes 10649600 | tf_op jit(solution)/shard_map/all_gather | solution.py:15
  997.8 7.0 copy-start.1
  1004.9 14.0 %copy-start.14 = (f32[136,2,1024]{2,1,0:T(2,128)S(1)}, f32[136,2,1024]{2,1,0:T(2,128)}, u32[]{:S(2)}) copy-start(f32[136,2,1024]{2,1,0:T(2,128)} %get-tuple-element.1102) | copy-start | bytes 3342340
  1027.7 7.6 slice-start
  1027.7 7.6 copy-start.12
  1048.0 41.0 %copy-start.26 = (f32[128]{0:T(128)S(1)}, f32[128]{0:T(128)}, u32[]{:S(2)}) copy-start(f32[128]{0:T(128)} %copy-done.25) | copy-start | bytes 1540
  1048.1 41.0 %copy-start.28 = (f32[128]{0:T(128)S(1)}, f32[128]{0:T(128)}, u32[]{:S(2)}) copy-start(f32[128]{0:T(128)} %copy-done.27) | copy-start | bytes 1540
  1048.3 40.7 %copy-start.4 = (f32[128,2560]{0,1:T(8,128)S(1)}, f32[128,2560]{0,1:T(8,128)}, u32[]{:S(2)}) copy-start(f32[128,2560]{0,1:T(8,128)} %copy-done.3) | copy-start | bytes 3932164
  1048.3 40.7 %copy-start.6 = (f32[2,2560]{0,1:T(8,128)S(1)}, f32[2,2560]{0,1:T(8,128)}, u32[]{:S(2)}) copy-start(f32[2,2560]{0,1:T(8,128)} %copy-done.5) | copy-start | bytes 61444
  1091.3 99.4 %copy-start.17 = (f32[2560]{0:T(1024)S(1)}, f32[2560]{0:T(1024)}, u32[]{:S(2)}) copy-start(f32[2560]{0:T(1024)} %copy-done.16) | copy-start | bytes 30724
  1091.3 99.4 %copy-start.19 = (f32[2560]{0:T(1024)S(1)}, f32[2560]{0:T(1024)}, u32[]{:S(2)}) copy-start(f32[2560]{0:T(1024)} %copy-done.18) | copy-start | bytes 30724
  1091.3 99.4 %copy-start.21 = (f32[2560]{0:T(1024)S(1)}, f32[2560]{0:T(1024)}, u32[]{:S(2)}) copy-start(f32[2560]{0:T(1024)} %copy-done.20) | copy-start | bytes 30724
  1091.3 99.4 %copy-start.30 = (f32[128]{0:T(128)S(1)}, f32[128]{0:T(128)}, u32[]{:S(2)}) copy-start(f32[128]{0:T(128)} %get-tuple-element.1110) | copy-start | bytes 1540
  1091.3 99.4 %copy-start.31 = (f32[128]{0:T(128)S(1)}, f32[128]{0:T(128)}, u32[]{:S(2)}) copy-start(f32[128]{0:T(128)} %get-tuple-element.1112) | copy-start | bytes 1540
  1091.7 97.5 %collective-permute-start.1 = (f32[2,2560]{1,0:T(2,128)S(1)}, f32[2,2560]{1,0:T(2,128)S(1)}, u32[]{:S(2)}, u32[]{:S(2)}) collective-permute-start(f32[2,2560]{1,0:T(2,128)S(1)} %copy.144), channel_id=1, source_target_pairs={{1,0},{2,1},{3,2},{4,3},{5,4},{6,5},{7,6},{8,7},{9,8},{10,9},{11,1... | collective-permute-start | bytes 61448 | tf_op jit(solution)/shard_map/ppermute | solution.py:32
  (16 other events, 35.8 us)
Sparse Core Ops, SparseCore 0:
  84.0 91.8 all-gather.8
  590.8 88.6 all-gather.10
where the time goes:
time: 1220 us; the launch traced here: 1200 us
  other arithmetic  462 us (38%)
  blocking collectives  368 us (30%)
  local copies, waits for them, and re-layouts  129 us (11%)
  matrix products  118 us (10%)
  waiting for transfers between devices  69.8 us (6%)
  loops' own time  25.3 us (2%)
  starting transfers between devices  15.7 us (1%)
  between operations  15.7 us (1%)
    select_n x256, other arithmetic, lap(): return jax.tree.map(lambda a, b: jnp.where(reached, a, b), new, before)  301 us
    unnamed x1, blocking collectives  131 us
    all_gather x2, blocking collectives, carried_in(): everything = jax.tree.map(lambda part: lax.all_gather(part, axis), x)  101 us
    psum x1, blocking collectives, on_device(): grad_conv = lax.psum(weight_part, ('seq', 'head'))  95.5 us
    sub x128, other arithmetic, combine(): carry_keep = 1.0 - following[2]  78.9 us
    dynamic_update_slice x48, local copies, waits for them, and re-layouts, attention_grads(): forward_out = lax.scan(forward_block, (prefix[0], prefix[1]), indices)  55 us
    all_to_all x1, blocking collectives, on_device(): lax.all_to_all(grad_mixed, 'head', split_axis=0, concat_axis=1, tiled=True)  40.7 us
    all_gather x2, waiting for transfers between devices, carried_in(): everything = jax.tree.map(lambda part: lax.all_gather(part, axis), x)  36.5 us
  transfers between devices with their start and end apart: 6, of which 2 were waited for; matrix products, arithmetic and copies ran while one was open for 2% of the time, Pallas kernels for 0%

commit v1 on v0

--- a/solution.py
+++ b/solution.py
@@ -242,7 +242,7 @@
     grad_projected, weight_part = conv_backward(
         returned, trailing, projected, leading, conv_weight, token_offsets
     )
-    grad_conv = lax.psum(weight_part, ("seq", "head"))
+    grad_conv = lax.all_gather(weight_part, ("seq", "head")).sum(axis=0)
     return (grad_projected, grad_conv)
 
 

time: 1220 us -> 1250 us (1.025)
  waiting for transfers between devices: 69.8 us -> 193 us
  blocking collectives: 368 us -> 274 us
    all_gather x0 -> x1, waiting for transfers between devices: none -> 120 us  [on_device(): grad_conv = lax.all_gather(weight_part, ('seq', 'head')).sum(axis=0)]
    psum x1 -> x0, blocking collectives: 95.5 us -> none  [on_device(): grad_conv = lax.psum(weight_part, ('seq', 'head'))]
    reduce_sum x0 -> x1, other arithmetic: none -> 12.6 us  [on_device(): grad_conv = lax.all_gather(weight_part, ('seq', 'head')).sum(axis=0)]
  transfers between devices with their start and end apart: 6 -> 7, of which waited for: 2 -> 4; matrix products, arithmetic and copies ran while one was open for 2% -> 2% of each run, Pallas kernels for 0% -> 0%
where the time goes in v1:
time: 1250 us; the launch traced here: 1240 us
  other arithmetic  464 us (37%)
  blocking collectives  274 us (22%)
  waiting for transfers between devices  193 us (15%)
  local copies, waits for them, and re-layouts  135 us (11%)
  matrix products  118 us (9%)
  loops' own time  25.9 us (2%)
  starting transfers between devices  15.7 us (1%)
  between operations  15.3 us (1%)
    select_n x256, other arithmetic, lap(): return jax.tree.map(lambda a, b: jnp.where(reached, a, b), new, before)  294 us
    unnamed x1, blocking collectives  132 us
    all_gather x1, waiting for transfers between devices, on_device(): grad_conv = lax.all_gather(weight_part, ('seq', 'head')).sum(axis=0)  120 us
    all_gather x2, blocking collectives, carried_in(): everything = jax.tree.map(lambda part: lax.all_gather(part, axis), x)  101 us
    sub x128, other arithmetic, combine(): carry_keep = 1.0 - following[2]  75.4 us
    dynamic_update_slice x48, local copies, waits for them, and re-layouts, attention_grads(): forward_out = lax.scan(forward_block, (prefix[0], prefix[1]), indices)  54.8 us
    all_to_all x1, blocking collectives, on_device(): lax.all_to_all(grad_mixed, 'head', split_axis=0, concat_axis=1, tiled=True)  40.8 us
    all_gather x2, waiting for transfers between devices, carried_in(): everything = jax.tree.map(lambda part: lax.all_gather(part, axis), x)  36.4 us
  transfers between devices with their start and end apart: 7, of which 4 were waited for; matrix products, arithmetic and copies ran while one was open for 2% of the time, Pallas kernels for 0%

profile of v1, /device:TPU:1, one launch (start us, length us, event | category | flops | bytes accessed | tf_op | source)
XLA Modules:
  0.0 1240.6 jit_solution(9369790844008259987)
XLA Ops:
  20.1 6.1 all-to-all-start
  27.7 33.3 %all-to-all-done = f32[128,8,320]{0,2,1:T(8,128)S(1)} async-done(((f32[128,8,320]{0,2,1:T(8,128)}), f32[128,8,320]{0,2,1:T(8,128)S(1)}, u32[]{:S(2)}, u32[]{:S(2)}) %all-to-all-start) | async-done | bytes 1310752 | tf_op jit(solution)/shard_map/all_to_all | solution.py:235
  94.8 131.7 %all-reduce = f32[64]{0:T(128)S(1)} all-reduce(f32[64]{0:T(128)S(1)} %dynamic-update-slice), channel_id=1, replica_groups=mesh['seq'=64,'head'=8] {'seq'}, use_global_device_ids=true, to_apply=%add | all-reduce | flops 64 | bytes 512
  236.0 51.6 %all-gather.5 = f32[64,2,153]{2,1,0:T(2,128)S(1)} all-gather(f32[1,2,153]{2,1,0:T(2,128)S(1)} %copy.127), channel_id=3, replica_groups=mesh['seq'=64,'head'=8] {'seq'}, dimensions={0}, use_global_device_ids=true | all-gather | bytes 79560 | tf_op jit(solution)/shard_map/all_gather | solution.py:15
  287.6 187.7 %while.82 = (s32[]{:T(128)}, f32[2,153,128]{2,1,0:T(8,128)S(1)}, f32[2,153]{1,0:T(2,128)S(1)}, s32[]{:T(128)}, f32[64,2,153,128]{3,2,1,0:T(8,128)}, /*index=5*/f...) while((s32[]{:T(128)}, f32[2,153,128]{2,1,0:T(8,128)S(1)}, ...), condition=%wide.region_5.6_spmd.clone, body=%wide.region_4.5_spmd.clone.sunk | while | flops 157901 | bytes 473831 | solution.py:26
  476.6 110.1 %while.80 = (s32[]{:T(128)}, f32[2,153,128]{2,1,0:T(8,128)S(1)}, f32[2,153]{1,0:T(2,128)S(1)}, f32[8,128,2,128]{1,0,3,2:T(8,128)}, f32[8,2,128]{2,1,0:T(2,128)S(...) while((s32[]{:T(128)}, f32[2,153,128]{2,1,0:T(8,128)S(1)}, ...), condition=%wide.region_9.10_spmd.clone, body=%wide.region_6.9_spmd.clone.sunk | while | flops 231664960 | bytes 3280461 | solution.py:149
  480.6 4.7 dynamic_update_slice.74
  494.4 4.7 dynamic_update_slice.74
  508.2 4.7 dynamic_update_slice.74
  521.9 4.7 dynamic_update_slice.74
  535.7 4.7 dynamic_update_slice.74
  549.5 4.7 dynamic_update_slice.74
  597.1 49.5 %all-gather.6 = f32[64,2,153]{2,1,0:T(2,128)S(1)} all-gather(f32[1,2,153]{2,1,0:T(2,128)S(1)} %bitcast.284), channel_id=5, replica_groups=mesh['seq'=64,'head'=8] {'seq'}, dimensions={0}, use_global_device_ids=true | all-gather | bytes 79560 | tf_op jit(solution)/shard_map/all_gather | solution.py:15
  646.6 36.4 %all-gather.14.cloned.1.call-done = f32[128,153,128]{2,1,0:T(8,128)} async-done(((f32[2,153,128]{2,1,0:T(8,128)}), f32[128,153,128]{2,1,0:T(8,128)}) %all-gather.14.cloned.1.call-update) | async-done | bytes 10027024 | tf_op jit(solution)/shard_map/all_gather | solution.py:15
  683.0 184.7 %while.83 = (s32[]{:T(128)}, f32[2,153,128]{2,1,0:T(8,128)S(1)}, f32[2,153]{1,0:T(2,128)S(1)}, s32[]{:T(128)}, f32[64,2,153,128]{3,2,1,0:T(8,128)}, /*index=5*/f...) while((s32[]{:T(128)}, f32[2,153,128]{2,1,0:T(8,128)S(1)}, ...), condition=%wide.region_12.13_spmd.clone, body=%wide.region_11.12_spmd.clone.sunk | while | flops 157905 | bytes 473893 | solution.py:26
  871.2 113.0 %while.81 = (s32[]{:T(128)}, f32[2,153,128]{2,1,0:T(8,128)S(1)}, f32[2,153]{1,0:T(2,128)S(1)}, f32[8,2,153,128]{3,2,1,0:T(8,128)}, f32[8,2,153,128]{3,2,1,0:T(8,...) while((s32[]{:T(128)}, f32[2,153,128]{2,1,0:T(8,128)S(1)}, ...), condition=%wide.region_14.15_spmd.clone, body=%wide.region_13.14_spmd.clone.sunk | while | flops 462717824 | bytes 4866477 | solution.py:209
  992.7 5.9 fusion.90
  998.7 14.0 %scatter_fusion = f32[2,16,1024]{2,0,1:T(2,128)S(1)} fusion(f32[2,16,1024]{2,0,1:T(2,128)S(1)} %split.16, s32[136]{0:T(256)S(1)} %copy-done.16, f32[136,2,1024]{2,1,0:T(2,128)} %get-tuple-element.1103), kind=kCustom, calls=%fused_computation.4 | custom fusion | flops 278528 | bytes 3342880 | tf_op jit(solution)/shard_map/transpose(jvp())/scatter-add | solution.py:39
  1012.7 7.6 scatter_fusion.1
  1021.8 7.6 scatter_fusion.3
  1029.4 7.6 scatter_fusion.2
  1044.8 40.8 %all_to_all.51 = f32[8,128,320]{1,2,0:T(8,128)S(1)} all-to-all(f32[8,128,320]{1,2,0:T(8,128)S(1)} %copy.143), channel_id=1, replica_groups=mesh['seq'=64,'head'=8] {'head'}, dimensions={0} | all-to-all | bytes 2621440 | tf_op jit(solution)/shard_map/all_to_all | solution.py:240
  1100.8 120.5 %all-gather.16.cloned.1.call-done = f32[512,3,2560]{2,1,0:T(4,128)} async-done(((f32[1,3,2560]{2,1,0:T(4,128)}), f32[512,3,2560]{2,1,0:T(4,128)}) %all-gather.16.cloned.1.call-update) | async-done | bytes 15728656 | tf_op jit(solution)/shard_map/all_gather | solution.py:245
  1221.2 12.6 %reduce_sum.77 = f32[3,2560]{1,0:T(4,128)} reduce(f32[512,3,2560]{2,1,0:T(4,128)} %all-gather.16.cloned.1.call-done, f32[]{:T(128)} %constant.210.clone.1), dimensions={0}, to_apply=%region_22.23 | reduce | flops 3924480 | bytes 15759364 | tf_op jit(solution)/shard_map/reduce_sum | solution.py:245
  (815 shorter events, 646.1 us)
Async XLA Ops:
  8.1 8.5 collective-permute-start
  16.6 3.5 copy-start.3
  17.0 3.1 copy-start.5
  20.1 6.9 copy-start.17
  20.1 6.9 copy-start.16
  20.1 40.9 %all-to-all-start = ((f32[128,8,320]{0,2,1:T(8,128)}), f32[128,8,320]{0,2,1:T(8,128)S(1)}, u32[]{:S(2)}, u32[]{:S(2)}) async-start(f32[128,8,320]{0,2,1:T(8,128)} %bitcast.267), calls=%async_computation | async-start | bytes 2621440 | tf_op jit(solution)/shard_map/all_to_all | solution.py:235
  26.2 261.4 %all-gather.12.cloned.1.call-start = ((), (), s32[]{:S(2)}) async-start(), calls=%async_computation.3 | async-start | bytes 10649600 | tf_op jit(solution)/shard_map/all_gather | solution.py:15
  26.3 66.4 %copy-start.15 = (s32[1026]{0:T(1024)}, s32[1026]{0:T(1024)S(1)}, u32[]{:S(2)}) copy-start(s32[1026]{0:T(1024)S(1)} %select_reduce_fusion) | copy-start | bytes 12316
  73.9 3.1 copy-start.18
  84.7 2.3 copy-start.14
  88.4 138.1 %all-to-all-start.1 = ((f32[128,8,256]{0,2,1:T(8,128)}), f32[128,8,256]{0,2,1:T(8,128)S(1)}, u32[]{:S(2)}, u32[]{:S(2)}) async-start(f32[128,8,256]{0,2,1:T(8,128)} %bitcast.275), calls=%async_computation.1 | async-start | bytes 2097152 | tf_op jit(solution)/shard_map/all_to_all | solution.py:236
  91.9 591.0 %all-gather.14.cloned.1.call-start = ((), (), s32[]{:S(2)}) async-start(), calls=%async_computation.4 | async-start | bytes 10649600 | tf_op jit(solution)/shard_map/all_gather | solution.py:15
  230.5 1.7 copy-start.10
  589.0 2.9 copy-start.2
  594.2 627.0 %all-gather.16.cloned.1.call-start = ((), (), s32[]{:S(2)}) async-start(), calls=%async_computation.5 | async-start | bytes 21012480 | tf_op jit(solution)/shard_map/all_gather | solution.py:245
  986.2 1.7 copy-start.8
  989.7 3.1 copy-start.7
  991.6 7.0 copy-start.1
  998.6 14.0 %copy-start.13 = (f32[136,2,1024]{2,1,0:T(2,128)S(1)}, f32[136,2,1024]{2,1,0:T(2,128)}, u32[]{:S(2)}) copy-start(f32[136,2,1024]{2,1,0:T(2,128)} %get-tuple-element.1102) | copy-start | bytes 3342340
  1021.7 7.6 slice-start
  1021.7 7.6 copy-start.11
  1044.8 40.9 %copy-start.4 = (f32[128,2560]{0,1:T(8,128)S(1)}, f32[128,2560]{0,1:T(8,128)}, u32[]{:S(2)}) copy-start(f32[128,2560]{0,1:T(8,128)} %copy-done.3) | copy-start | bytes 3932164
  1044.8 40.8 %copy-start.6 = (f32[2,2560]{0,1:T(8,128)S(1)}, f32[2,2560]{0,1:T(8,128)}, u32[]{:S(2)}) copy-start(f32[2,2560]{0,1:T(8,128)} %copy-done.5) | copy-start | bytes 61444
  1088.9 4.5 collective-permute-start.1
  (4 other events, 5.0 us)
Sparse Core Ops, SparseCore 0:
  87.2 91.7 all-gather.11
  594.3 88.6 all-gather.13
  1088.6 132.5 all-gather.15
